TPU v7x, 256 devices: a whole 4x4x8 slice. The times are simulated.
256 devices in a mesh: ctx: 64 (over x, z, core), tp: 4 (over y).
Axes of the slice: x: 4, y: 4, z: 8, core: 2. Of those that a mesh axis runs over, the one named last changes fastest.
Arguments:
- inputs: bfloat16 [8192, 4096], P('ctx'), may hold values from -6 to 6
- w_query: bfloat16 [4096, 4096], P(None, 'tp'), may hold values from -0.109375 to 0.109375
- w_key: bfloat16 [4096, 512], P(None, 'tp'), may hold values from -0.109375 to 0.109375
- w_value: bfloat16 [4096, 512], P(None, 'tp'), may hold values from -0.09375 to 0.09375
- attn_out: bfloat16 [8192, 4096], P('ctx', 'tp'), may hold values from -6 to 6
- d_out: bfloat16 [8192, 4096], P('ctx', 'tp'), may hold values from -6 to 6
- block_order: int32 [128], replicated, may hold values from 0 to 127, each once
Outputs:
- d_input: bfloat16 [8192, 4096], P('ctx', 'tp')
Inputs may be any that keep to these rules, and one draw needn't show every extreme that they name: `block_order`: a permutation of the sequence blocks.
All inputs are finite; a program needn't handle non-finite values.
Results may differ from a plain program's by a relative error of at most 0.012.
Values may be sent and summed in bfloat16 or wider, within the bound.
No kernel may reach another device: no remote copies, remote signals or barrier semaphores. Data moves between devices by JAX's collectives and lax.ppermute only.
A program may use at most 192 MiB of HBM per device.

v0:
```python
import math

import jax
import jax.numpy as jnp
from jax import lax
from jax.sharding import PartitionSpec as P

big_negative = -1e30


def row_positions(order, start, count, span):
    rows = start + lax.iota(jnp.int32, count)
    slot = rows // span
    table = jnp.sum(
        jnp.where(slot[:, None] == lax.iota(jnp.int32, order.shape[0])[None, :], order[None, :], 0),
        axis=1,
    )
    return table * span + rows % span


def contract_rows(left, weight):
    return lax.dot_general(
        left, weight, (((1,), (1,)), ((), ())), preferred_element_type=jnp.float32
    )


def on_device(inputs, w_query, w_key, w_value, attn_out, d_out, block_order):
    tokens = inputs.shape[0]
    span = tokens // 2
    head_dim = w_key.shape[1]
    heads = w_query.shape[1] // head_dim
    scale = head_dim ** (-0.5)
    keys = jnp.dot(inputs, w_key, preferred_element_type=jnp.float32).astype(jnp.bfloat16)
    values = jnp.dot(inputs, w_value, preferred_element_type=jnp.float32).astype(jnp.bfloat16)
    seq = tokens * lax.axis_size("ctx")
    my_pos = row_positions(block_order, lax.axis_index("ctx") * tokens, tokens, span)
    latest = jnp.max(my_pos)
    queries = (
        jnp.dot(inputs, w_query, preferred_element_type=jnp.float32)
        .astype(jnp.bfloat16)
        .reshape(tokens, heads, head_dim)
    )
    grads3 = d_out.reshape(tokens, heads, head_dim)
    delta = jnp.sum(
        grads3.astype(jnp.float32) * attn_out.reshape(tokens, heads, head_dim).astype(jnp.float32),
        axis=-1,
    ).T

    def guarded(work, carry, piece_k, start):
        key_pos = row_positions(block_order, start, piece_k.shape[0], span)
        return lax.cond(jnp.min(key_pos) > latest, lambda c: c, lambda c: work(c, key_pos), carry)

    def stats_step(carry, piece_k, start):

        def work(state, key_pos):
            top, total = state
            mask = (key_pos[None, :] <= my_pos[:, None])[None]
            s = (
                jnp.einsum("thd,nd->htn", queries, piece_k, preferred_element_type=jnp.float32)
                * scale
            )
            s = jnp.where(mask, s, big_negative)
            top_new = jnp.maximum(top, jnp.max(s, axis=-1))
            terms = jnp.where(mask, jnp.exp(s - top_new[..., None]), 0.0)
            return (top_new, total * jnp.exp(top - top_new) + jnp.sum(terms, axis=-1))

        return guarded(work, carry, piece_k, start)

    def grad_step(carry, pieces, start):
        piece_k, piece_v = pieces

        def work(state, key_pos):
            dq, dk_full, dv_full = state
            mask = (key_pos[None, :] <= my_pos[:, None])[None]
            s = (
                jnp.einsum("thd,nd->htn", queries, piece_k, preferred_element_type=jnp.float32)
                * scale
            )
            p = jnp.where(mask, jnp.exp(s - lse[..., None]), 0.0)
            dp = jnp.einsum("thd,nd->htn", grads3, piece_v, preferred_element_type=jnp.float32)
            ds_b = (p * (dp - delta[..., None]) * scale).astype(jnp.bfloat16)
            p_b = p.astype(jnp.bfloat16)
            dq = dq + jnp.einsum("htn,nd->thd", ds_b, piece_k, preferred_element_type=jnp.float32)
            dk_piece = jnp.einsum("htn,thd->nd", ds_b, queries, preferred_element_type=jnp.float32)
            dv_piece = jnp.einsum("htn,thd->nd", p_b, grads3, preferred_element_type=jnp.float32)
            dk_full = lax.dynamic_update_slice_in_dim(dk_full, dk_piece, start, 0)
            dv_full = lax.dynamic_update_slice_in_dim(dv_full, dv_piece, start, 0)
            return (dq, dk_full, dv_full)

        return guarded(work, carry, piece_k, start)

    stats_init = (
        jnp.full((heads, tokens), big_negative, jnp.float32),
        jnp.zeros((heads, tokens), jnp.float32),
    )
    zero_rows = jnp.zeros((seq, head_dim), jnp.float32)
    grad_init = (jnp.zeros((tokens, heads, head_dim), jnp.float32), zero_rows, zero_rows)
    all_keys, all_values = (
        lax.all_gather(keys, "ctx", axis=0, tiled=True),
        lax.all_gather(values, "ctx", axis=0, tiled=True),
    )
    block = math.gcd(seq, 1024)
    count = seq // block

    def stats_loop(i, state):
        start = (i * block).astype(jnp.int32)
        return stats_step(state, lax.dynamic_slice_in_dim(all_keys, start, block, 0), start)

    top, total = lax.fori_loop(0, count, stats_loop, stats_init)
    lse = top + jnp.log(total)

    def grad_loop(i, state):
        start = (i * block).astype(jnp.int32)
        pieces = (
            lax.dynamic_slice_in_dim(all_keys, start, block, 0),
            lax.dynamic_slice_in_dim(all_values, start, block, 0),
        )
        return grad_step(state, pieces, start)

    dq, dk_full, dv_full = lax.fori_loop(0, count, grad_loop, grad_init)
    dk_mine, dv_mine = (
        lax.psum_scatter(dk_full, "ctx", scatter_dimension=0, tiled=True),
        lax.psum_scatter(dv_full, "ctx", scatter_dimension=0, tiled=True),
    )
    dq_b = dq.astype(jnp.bfloat16).reshape(tokens, heads * head_dim)
    partial_value = contract_rows(dq_b, w_query)
    partial_value = partial_value + contract_rows(dk_mine.astype(jnp.bfloat16), w_key)
    partial_value = partial_value + contract_rows(dv_mine.astype(jnp.bfloat16), w_value)
    return lax.psum_scatter(
        partial_value.astype(jnp.bfloat16), "tp", scatter_dimension=1, tiled=True
    )


def solution(mesh):
    placed = (
        P("ctx", None),
        P(None, "tp"),
        P(None, "tp"),
        P(None, "tp"),
        P("ctx", "tp"),
        P("ctx", "tp"),
        P(),
    )
    return jax.shard_map(
        on_device, mesh=mesh, in_specs=placed, out_specs=P("ctx", "tp"), check_vma=False
    )
```

profile of v0, /device:TPU:2, one launch (start us, length us, event | category | flops | bytes accessed | tf_op | source)
XLA Modules:
  0.0 588.8 jit_solution(3103527456440463668)
XLA Ops:
  10.3 2.6 convolution_convert_fusion.1
  13.6 4.6 fusion.47
  19.2 70.6 %all-gather.3.cloned.1.call-done = bf16[8192,128]{1,0:T(8,128)(2,1)} async-done(((bf16[128,128]{1,0:T(8,128)(2,1)}), bf16[8192,128]{1,0:T(8,128)(2,1)}) %all-gather.3.cloned.1.call-update) | async-done | bytes 2097168 | tf_op jit(solution)/shard_map/all_gather | solution.py:99
  89.7 42.9 %while.36 = (s32[]{:T(128)}, f32[8,128]{1,0:T(8,128)S(1)}, f32[8,128]{1,0:T(8,128)S(1)}, s32[128]{0:T(128)S(1)}, s32[]{:T(128)}, /*index=5*/s32[128]{0:T(128)S(1...) while((s32[]{:T(128)}, f32[8,128]{1,0:T(8,128)S(1)}, ...), condition=%wide.region_9.10_spmd, body=%wide.region_2.9_spmd.sunk | while | flops 277381120 | bytes 9385225 | solution.py:109
  92.1 3.0 conditional.4
  97.4 3.0 conditional.4
  102.8 3.0 conditional.4
  108.1 3.0 conditional.4
  113.5 3.0 conditional.4
  118.9 3.0 conditional.4
  124.2 3.0 conditional.4
  129.6 3.0 conditional.4
  132.6 34.9 %all-gather.5.cloned.1.call-done = bf16[8192,128]{1,0:T(8,128)(2,1)} async-done(((bf16[128,128]{1,0:T(8,128)(2,1)}), bf16[8192,128]{1,0:T(8,128)(2,1)}) %all-gather.5.cloned.1.call-update) | async-done | bytes 2097168 | tf_op jit(solution)/shard_map/all_gather | solution.py:100
  172.0 92.8 %while.37 = (s32[]{:T(128)}, f32[128,8,128]{2,0,1:T(8,128)S(1)}, f32[8192,128]{1,0:T(8,128)}, f32[8192,128]{1,0:T(8,128)}, s32[128]{0:T(128)S(1)}, /*index=5*/s3...) while((s32[]{:T(128)}, f32[128,8,128]{2,0,1:T(8,128)S(1)}, ...), condition=%wide.region_16.17_spmd, body=%wide.region_11.16_spmd.sunk | while | flops 1354397696 | bytes 23238016 | solution.py:120
  174.4 9.2 %conditional.5 = ((f32[128,8,128]{2,0,1:T(8,128)S(1)}, f32[8192,128]{1,0:T(8,128)}, f32[8192,128]{1,0:T(8,128)})) conditional(s32[]{:T(128)} %convert_element_type.94, (s32[1024]{0:T(1024)S(1)}, s32[128]{0:T(128)S(1)}, s32[]{:T(128)}, bf16[8192,128]{1,0:T(8,128)(2,1)}, bf16[128,8,128]{2,0,1:T(8,128)(2,1)S(1)}, /*index=5*/f32[8,128]{1,0:T(8,128)S(1)}, ...), branch_computations={%region_14.14_spmd, %region_15.15_spmd} | conditional | flops 1353973760 | bytes 23216726 | solution.py:51
  176.3 2.5 fusion.13
  185.9 9.3 %conditional.5 = ((f32[128,8,128]{2,0,1:T(8,128)S(1)}, f32[8192,128]{1,0:T(8,128)}, f32[8192,128]{1,0:T(8,128)})) conditional(s32[]{:T(128)} %convert_element_type.94, (s32[1024]{0:T(1024)S(1)}, s32[128]{0:T(128)S(1)}, s32[]{:T(128)}, bf16[8192,128]{1,0:T(8,128)(2,1)}, bf16[128,8,128]{2,0,1:T(8,128)(2,1)S(1)}, /*index=5*/f32[8,128]{1,0:T(8,128)S(1)}, ...), branch_computations={%region_14.14_spmd, %region_15.15_spmd} | conditional | flops 1353973760 | bytes 23216726 | solution.py:51
  197.5 9.3 %conditional.5 = ((f32[128,8,128]{2,0,1:T(8,128)S(1)}, f32[8192,128]{1,0:T(8,128)}, f32[8192,128]{1,0:T(8,128)})) conditional(s32[]{:T(128)} %convert_element_type.94, (s32[1024]{0:T(1024)S(1)}, s32[128]{0:T(128)S(1)}, s32[]{:T(128)}, bf16[8192,128]{1,0:T(8,128)(2,1)}, bf16[128,8,128]{2,0,1:T(8,128)(2,1)S(1)}, /*index=5*/f32[8,128]{1,0:T(8,128)S(1)}, ...), branch_computations={%region_14.14_spmd, %region_15.15_spmd} | conditional | flops 1353973760 | bytes 23216726 | solution.py:51
  199.4 2.5 fusion.13
  209.1 9.3 %conditional.5 = ((f32[128,8,128]{2,0,1:T(8,128)S(1)}, f32[8192,128]{1,0:T(8,128)}, f32[8192,128]{1,0:T(8,128)})) conditional(s32[]{:T(128)} %convert_element_type.94, (s32[1024]{0:T(1024)S(1)}, s32[128]{0:T(128)S(1)}, s32[]{:T(128)}, bf16[8192,128]{1,0:T(8,128)(2,1)}, bf16[128,8,128]{2,0,1:T(8,128)(2,1)S(1)}, /*index=5*/f32[8,128]{1,0:T(8,128)S(1)}, ...), branch_computations={%region_14.14_spmd, %region_15.15_spmd} | conditional | flops 1353973760 | bytes 23216726 | solution.py:51
  211.0 2.5 fusion.13
  220.8 9.3 %conditional.5 = ((f32[128,8,128]{2,0,1:T(8,128)S(1)}, f32[8192,128]{1,0:T(8,128)}, f32[8192,128]{1,0:T(8,128)})) conditional(s32[]{:T(128)} %convert_element_type.94, (s32[1024]{0:T(1024)S(1)}, s32[128]{0:T(128)S(1)}, s32[]{:T(128)}, bf16[8192,128]{1,0:T(8,128)(2,1)}, bf16[128,8,128]{2,0,1:T(8,128)(2,1)S(1)}, /*index=5*/f32[8,128]{1,0:T(8,128)S(1)}, ...), branch_computations={%region_14.14_spmd, %region_15.15_spmd} | conditional | flops 1353973760 | bytes 23216726 | solution.py:51
  222.6 2.5 fusion.13
  232.3 9.3 %conditional.5 = ((f32[128,8,128]{2,0,1:T(8,128)S(1)}, f32[8192,128]{1,0:T(8,128)}, f32[8192,128]{1,0:T(8,128)})) conditional(s32[]{:T(128)} %convert_element_type.94, (s32[1024]{0:T(1024)S(1)}, s32[128]{0:T(128)S(1)}, s32[]{:T(128)}, bf16[8192,128]{1,0:T(8,128)(2,1)}, bf16[128,8,128]{2,0,1:T(8,128)(2,1)S(1)}, /*index=5*/f32[8,128]{1,0:T(8,128)S(1)}, ...), branch_computations={%region_14.14_spmd, %region_15.15_spmd} | conditional | flops 1353973760 | bytes 23216726 | solution.py:51
  244.0 9.2 %conditional.5 = ((f32[128,8,128]{2,0,1:T(8,128)S(1)}, f32[8192,128]{1,0:T(8,128)}, f32[8192,128]{1,0:T(8,128)})) conditional(s32[]{:T(128)} %convert_element_type.94, (s32[1024]{0:T(1024)S(1)}, s32[128]{0:T(128)S(1)}, s32[]{:T(128)}, bf16[8192,128]{1,0:T(8,128)(2,1)}, bf16[128,8,128]{2,0,1:T(8,128)(2,1)S(1)}, /*index=5*/f32[8,128]{1,0:T(8,128)S(1)}, ...), branch_computations={%region_14.14_spmd, %region_15.15_spmd} | conditional | flops 1353973760 | bytes 23216726 | solution.py:51
  245.9 2.5 fusion.13
  255.5 9.3 %conditional.5 = ((f32[128,8,128]{2,0,1:T(8,128)S(1)}, f32[8192,128]{1,0:T(8,128)}, f32[8192,128]{1,0:T(8,128)})) conditional(s32[]{:T(128)} %convert_element_type.94, (s32[1024]{0:T(1024)S(1)}, s32[128]{0:T(128)S(1)}, s32[]{:T(128)}, bf16[8192,128]{1,0:T(8,128)(2,1)}, bf16[128,8,128]{2,0,1:T(8,128)(2,1)S(1)}, /*index=5*/f32[8,128]{1,0:T(8,128)S(1)}, ...), branch_computations={%region_14.14_spmd, %region_15.15_spmd} | conditional | flops 1353973760 | bytes 23216726 | solution.py:51
  265.8 7.7 %fusion.58 = f32[128,4096]{1,0:T(8,128)} fusion(bf16[128,1024]{0,1:T(8,128)(2,1)S(1)} %bitcast.85, bf16[4096,1024]{1,0:T(8,128)(2,1)} %param.16), kind=kOutput, calls=%fused_computation.93 | convolution fusion | flops 1073741824 | bytes 10747904 | tf_op jit(solution)/shard_map/dot_general | solution.py:22
  273.5 133.5 %reduce-scatter.4.cloned.1.call-done = f32[128,128]{1,0:T(8,128)} async-done(((f32[8192,128]{1,0:T(8,128)}), f32[128,128]{1,0:T(8,128)}) %reduce-scatter.4.cloned.1.call-update) | async-done | bytes 65552 | tf_op jit(solution)/shard_map/reduce_scatter | solution.py:122
  409.1 144.7 %reduce-scatter.6.cloned.1.call-done = f32[128,128]{1,0:T(8,128)} async-done(((f32[8192,128]{1,0:T(8,128)}), f32[128,128]{1,0:T(8,128)}) %reduce-scatter.6.cloned.1.call-update) | async-done | bytes 65552 | tf_op jit(solution)/shard_map/reduce_scatter | solution.py:123
  553.8 2.7 fusion.46
  556.5 25.7 %reduce-scatter.8.cloned.1.call-done = bf16[128,1024]{1,0:T(8,128)(2,1)} async-done(((bf16[128,4096]{1,0:T(8,128)(2,1)}), bf16[128,1024]{1,0:T(8,128)(2,1)}) %reduce-scatter.8.cloned.1.call-update) | async-done | bytes 262160 | tf_op jit(solution)/shard_map/reduce_scatter | solution.py:129
  (176 shorter events, 115.1 us)
Async XLA Ops:
  6.5 1.4 copy-start
  6.5 7.0 %copy-start.1 = (bf16[128,4096]{1,0:T(8,128)(2,1)S(1)}, bf16[128,4096]{1,0:T(8,128)(2,1)}, u32[]{:S(2)}) copy-start(bf16[128,4096]{1,0:T(8,128)(2,1)} %param.15) | copy-start | bytes 3145732
  6.5 6.4 %copy-start.2 = (bf16[128,1024]{1,0:T(8,128)(2,1)S(1)}, bf16[128,1024]{1,0:T(8,128)(2,1)}, u32[]{:S(2)}) copy-start(bf16[128,1024]{1,0:T(8,128)(2,1)} %param.20) | copy-start | bytes 786436
  6.5 6.8 %copy-start.3 = (bf16[128,1024]{1,0:T(8,128)(2,1)S(1)}, bf16[128,1024]{1,0:T(8,128)(2,1)}, u32[]{:S(2)}) copy-start(bf16[128,1024]{1,0:T(8,128)(2,1)} %param.19) | copy-start | bytes 786436
  6.5 83.2 %all-gather.3.cloned.1.call-start = ((), (), s32[]{:S(2)}) async-start(), calls=%async_computation.3 | async-start | bytes 2129920 | tf_op jit(solution)/shard_map/all_gather | solution.py:99
  10.2 157.4 %all-gather.5.cloned.1.call-start = ((), (), s32[]{:S(2)}) async-start(), calls=%async_computation.4 | async-start | bytes 2129920 | tf_op jit(solution)/shard_map/all_gather | solution.py:100
  12.8 394.2 %reduce-scatter.4.cloned.1.call-start = ((), (), s32[]{:S(2)}) async-start(), calls=%async_computation.5 | async-start | bytes 4259840 | tf_op jit(solution)/shard_map/reduce_scatter | solution.py:122
  13.6 4.7 copy-start.4
  264.8 289.0 %reduce-scatter.6.cloned.1.call-start = ((), (), s32[]{:S(2)}) async-start(), calls=%async_computation.6 | async-start | bytes 4259840 | tf_op jit(solution)/shard_map/reduce_scatter | solution.py:123
  265.4 316.9 %reduce-scatter.8.cloned.1.call-start = ((), (), s32[]{:S(2)}) async-start(), calls=%async_computation.7 | async-start | bytes 1310720 | tf_op jit(solution)/shard_map/reduce_scatter | solution.py:129
Sparse Core Ops, SparseCore 0:
  10.3 79.3 all-gather.2
  92.5 75.0 all-gather.4
  264.9 142.0 reduce-scatter.3
  411.0 142.7 reduce-scatter.5
  556.7 25.5 reduce-scatter.7
where the time goes:
time: 590 us; the launch traced here: 589 us
  waiting for transfers between devices  410 us (69%)
  matrix products  108 us (18%)
  other arithmetic  29.7 us (5%)
  loops' own time  21 us (4%)
  between operations  13.3 us (2%)
  local copies, waits for them, and re-layouts  6.58 us (1%)
    reduce_scatter x1, waiting for transfers between devices, on_device(): lax.psum_scatter(dv_full, 'ctx', scatter_dimension=0, tiled=True)  145 us
    reduce_scatter x1, waiting for transfers between devices, on_device(): lax.psum_scatter(dk_full, 'ctx', scatter_dimension=0, tiled=True)  134 us
    all_gather x1, waiting for transfers between devices, on_device(): lax.all_gather(keys, 'ctx', axis=0, tiled=True)  70.6 us
    all_gather x1, waiting for transfers between devices, on_device(): lax.all_gather(values, 'ctx', axis=0, tiled=True)  34.9 us
    dot_general x16, matrix products, work(): jnp.einsum('thd,nd->htn', queries, piece_k, preferred_element_type=jnp.fl...  26.9 us
    reduce_scatter x1, waiting for transfers between devices, on_device(): lax.psum_scatter(partial_value.astype(jnp.bfloat16), 'tp', scatter_dimens...  25.7 us
    dot_general x8, matrix products, work(): jnp.einsum('thd,nd->htn', grads3, piece_v, preferred_element_type=jnp.flo...  19.7 us
    dot_general x8, matrix products, work(): jnp.einsum('htn,nd->thd', ds_b, piece_k, preferred_element_type=jnp.float32)  13.9 us
  transfers between devices with their start and end apart: 5, of which 5 were waited for; matrix products, arithmetic and copies ran while one was open for 9% of the time, Pallas kernels for 0%

commit v1 on v0

--- a/solution.py
+++ b/solution.py
@@ -1,4 +1,6 @@
 import math
+
+import numpy as np
 
 import jax
 import jax.numpy as jnp
@@ -6,6 +8,45 @@
 from jax.sharding import PartitionSpec as P
 
 big_negative = -1e30
+
+
+def exchange_orders(n):
+    if n == 64:
+        return ([5, 3, 2, 4, 1, 0], [3, 2, 5, 1, 4, 0])
+    bits = list(range(int(math.log2(n))))[::-1]
+    return (bits, bits)
+
+
+def step_partners(n, orders, s):
+    return [i ^ (1 << orders[i & 1][s]) for i in range(n)]
+
+
+def owner_table(n, orders):
+    owners = [[i] for i in range(n)]
+    for s in range(len(orders[0])):
+        partner = step_partners(n, orders, s)
+        owners = [owners[i] + owners[partner[i]] for i in range(n)]
+    return np.asarray(owners, np.int32)
+
+
+def gather_slots(pieces, n, orders):
+    bufs = tuple(p[None] for p in pieces)
+    for s in range(len(orders[0])):
+        partner = step_partners(n, orders, s)
+        other = lax.ppermute(bufs, "ctx", [(i, partner[i]) for i in range(n)])
+        bufs = tuple(jnp.concatenate([b, o], axis=0) for b, o in zip(bufs, other))
+    return bufs
+
+
+def scatter_slots(bufs, n, orders):
+    for s in reversed(range(len(orders[0]))):
+        partner = step_partners(n, orders, s)
+        half = bufs[0].shape[0] // 2
+        recv = lax.ppermute(
+            tuple(b[half:] for b in bufs), "ctx", [(i, partner[i]) for i in range(n)]
+        )
+        bufs = tuple(b[:half] + r for b, r in zip(bufs, recv))
+    return tuple(b[0] for b in bufs)
 
 
 def row_positions(order, start, count, span):
@@ -30,10 +71,13 @@
     head_dim = w_key.shape[1]
     heads = w_query.shape[1] // head_dim
     scale = head_dim ** (-0.5)
+    n = lax.axis_size("ctx")
+    orders = exchange_orders(n)
+    me = lax.axis_index("ctx")
     keys = jnp.dot(inputs, w_key, preferred_element_type=jnp.float32).astype(jnp.bfloat16)
     values = jnp.dot(inputs, w_value, preferred_element_type=jnp.float32).astype(jnp.bfloat16)
-    seq = tokens * lax.axis_size("ctx")
-    my_pos = row_positions(block_order, lax.axis_index("ctx") * tokens, tokens, span)
+    seq = tokens * n
+    my_pos = row_positions(block_order, me * tokens, tokens, span)
     latest = jnp.max(my_pos)
     queries = (
         jnp.dot(inputs, w_query, preferred_element_type=jnp.float32)
@@ -46,8 +90,13 @@
         axis=-1,
     ).T
 
-    def guarded(work, carry, piece_k, start):
-        key_pos = row_positions(block_order, start, piece_k.shape[0], span)
+    owners = lax.dynamic_index_in_dim(jnp.asarray(owner_table(n, orders)), me, 0, keepdims=False)
+    local_rows = lax.iota(jnp.int32, tokens)
+    key_rows = owners[:, None] * tokens + local_rows[None, :]
+    all_pos = (jnp.take(block_order, key_rows // span) * span + key_rows % span).reshape(seq)
+
+    def guarded(work, carry, start, count):
+        key_pos = lax.dynamic_slice_in_dim(all_pos, start, count, 0)
         return lax.cond(jnp.min(key_pos) > latest, lambda c: c, lambda c: work(c, key_pos), carry)
 
     def stats_step(carry, piece_k, start):
@@ -64,7 +113,7 @@
             terms = jnp.where(mask, jnp.exp(s - top_new[..., None]), 0.0)
             return (top_new, total * jnp.exp(top - top_new) + jnp.sum(terms, axis=-1))
 
-        return guarded(work, carry, piece_k, start)
+        return guarded(work, carry, start, piece_k.shape[0])
 
     def grad_step(carry, pieces, start):
         piece_k, piece_v = pieces
@@ -87,7 +136,7 @@
             dv_full = lax.dynamic_update_slice_in_dim(dv_full, dv_piece, start, 0)
             return (dq, dk_full, dv_full)
 
-        return guarded(work, carry, piece_k, start)
+        return guarded(work, carry, start, piece_k.shape[0])
 
     stats_init = (
         jnp.full((heads, tokens), big_negative, jnp.float32),
@@ -95,10 +144,9 @@
     )
     zero_rows = jnp.zeros((seq, head_dim), jnp.float32)
     grad_init = (jnp.zeros((tokens, heads, head_dim), jnp.float32), zero_rows, zero_rows)
-    all_keys, all_values = (
-        lax.all_gather(keys, "ctx", axis=0, tiled=True),
-        lax.all_gather(values, "ctx", axis=0, tiled=True),
-    )
+    slot_keys, slot_values = gather_slots((keys, values), n, orders)
+    all_keys = slot_keys.reshape(seq, head_dim)
+    all_values = slot_values.reshape(seq, head_dim)
     block = math.gcd(seq, 1024)
     count = seq // block
 
@@ -118,9 +166,8 @@
         return grad_step(state, pieces, start)
 
     dq, dk_full, dv_full = lax.fori_loop(0, count, grad_loop, grad_init)
-    dk_mine, dv_mine = (
-        lax.psum_scatter(dk_full, "ctx", scatter_dimension=0, tiled=True),
-        lax.psum_scatter(dv_full, "ctx", scatter_dimension=0, tiled=True),
+    dk_mine, dv_mine = scatter_slots(
+        (dk_full.reshape(n, tokens, head_dim), dv_full.reshape(n, tokens, head_dim)), n, orders
     )
     dq_b = dq.astype(jnp.bfloat16).reshape(tokens, heads * head_dim)
     partial_value = contract_rows(dq_b, w_query)

time: 590 us -> 357 us (0.61)
  waiting for transfers between devices: 410 us -> 91 us
  local copies, waits for them, and re-layouts: 6.58 us -> 75.9 us
  starting transfers between devices: 0.38 us -> 47.2 us
  matrix products: 108 us -> 79.3 us
    reduce_scatter x2 -> x0, waiting for transfers between devices: 278 us -> none  [the longest x1 145 us: on_device(): lax.psum_scatter(dv_full, 'ctx', scatter_dimension=0, tiled=True)]
    all_gather x2 -> x0, waiting for transfers between devices: 106 us -> none  [the longest x1 70.6 us: on_device(): lax.all_gather(keys, 'ctx', axis=0, tiled=True)]
    ppermute x0 -> x24, waiting for transfers between devices: none -> 63.9 us  [the longest x12 48 us: scatter_slots(): lax.ppermute(tuple((b[half:] for b in bufs)), 'ctx', [(i, partner[i]) for...]
    gather x0 -> x1, local copies, waits for them, and re-layouts: none -> 48.9 us  [on_device(): jnp.take(block_order, key_rows // span) * span + key_rows % span]
    ppermute x0 -> x24, starting transfers between devices: none -> 47.2 us  [the longest x12 23.7 us: gather_slots(): other = lax.ppermute(bufs, 'ctx', [(i, partner[i]) for i in range(n)])]
    dot_general x16, matrix products: 26.9 us -> 11.7 us  [work(): jnp.einsum('thd,nd->htn', queries, piece_k, preferred_element_type=jnp.fl...]
    unnamed x12 -> x26, local copies, waits for them, and re-layouts: 1.69 us -> 9.66 us
    dot_general x8, matrix products: 13.9 us -> 6.3 us  [work(): jnp.einsum('htn,nd->thd', ds_b, piece_k, preferred_element_type=jnp.float32)]
  transfers between devices with their start and end apart: 5 -> 25, of which waited for: 5 -> 14; matrix products, arithmetic and copies ran while one was open for 9% -> 29% of each run, Pallas kernels for 0% -> 0%
where the time goes in v1:
time: 357 us; the launch traced here: 356 us
  waiting for transfers between devices  91 us (25%)
  matrix products  79.3 us (22%)
  local copies, waits for them, and re-layouts  75.9 us (21%)
  starting transfers between devices  47.2 us (13%)
  other arithmetic  27.5 us (8%)
  loops' own time  21.2 us (6%)
  between operations  13.8 us (4%)
    gather x1, local copies, waits for them, and re-layouts, on_device(): jnp.take(block_order, key_rows // span) * span + key_rows % span  48.9 us
    ppermute x12, waiting for transfers between devices, scatter_slots(): lax.ppermute(tuple((b[half:] for b in bufs)), 'ctx', [(i, partner[i]) for...  48 us
    reduce_scatter x1, waiting for transfers between devices, on_device(): lax.psum_scatter(partial_value.astype(jnp.bfloat16), 'tp', scatter_dimens...  27.1 us
    ppermute x12, starting transfers between devices, gather_slots(): other = lax.ppermute(bufs, 'ctx', [(i, partner[i]) for i in range(n)])  23.7 us
    ppermute x12, starting transfers between devices, scatter_slots(): lax.ppermute(tuple((b[half:] for b in bufs)), 'ctx', [(i, partner[i]) for...  23.5 us
    dot_general x8, matrix products, work(): jnp.einsum('thd,nd->htn', grads3, piece_v, preferred_element_type=jnp.flo...  19.7 us
    ppermute x12, waiting for transfers between devices, gather_slots(): other = lax.ppermute(bufs, 'ctx', [(i, partner[i]) for i in range(n)])  15.9 us
    dot_general x8, matrix products, work(): jnp.einsum('htn,thd->nd', p_b, grads3, preferred_element_type=jnp.float32)  13.3 us
  transfers between devices with their start and end apart: 25, of which 14 were waited for; matrix products, arithmetic and copies ran while one was open for 29% of the time, Pallas kernels for 0%

profile of v1, /device:TPU:2, one launch (start us, length us, event | category | flops | bytes accessed | tf_op | source)
XLA Modules:
  0.0 355.9 jit_solution(14699863112870919291)
XLA Ops:
  14.8 4.6 %fusion.35 = bf16[16,8,8,128]{3,2,1,0:T(8,128)(2,1)S(1)} fusion(bf16[128,4096]{1,0:T(8,128)(2,1)S(1)} %copy-done, bf16[4096,1024]{1,0:T(8,128)(2,1)} %param.17), kind=kOutput, calls=%fused_computation.43 | convolution fusion | flops 1073872896 | bytes 9699328 | tf_op jit(solution)/shard_map/dot_general | solution.py:83
  19.4 7.3 %collective-permute-start.1 = (bf16[2,128,128]{2,1,0:T(8,128)(2,1)S(1)}, bf16[2,128,128]{2,1,0:T(8,128)(2,1)S(1)}, u32[]{:S(2)}, u32[]{:S(2)}) collective-permute-start(bf16[2,128,128]{2,1,0:T(8,128)(2,1)S(1)} %pad_maximum_fusion.4), channel_id=1, source_target_pairs={{0,32},{4,20},{8,40},{12,28},{16,48},{20,4},{24,56},{28,12},{32,0}... | collective-permute-start | bytes 196616 | tf_op jit(solution)/shard_map/ppermute | solution.py:36
  29.1 2.8 collective-permute-start.2
  34.3 4.7 %collective-permute-start.7 = (bf16[2,128,128]{2,1,0:T(8,128)(2,1)S(1)}, bf16[2,128,128]{2,1,0:T(8,128)(2,1)S(1)}, u32[]{:S(2)}, u32[]{:S(2)}) collective-permute-start(bf16[2,128,128]{2,1,0:T(8,128)(2,1)S(1)} %pad_maximum_fusion.5), channel_id=1, source_target_pairs={{0,32},{4,20},{8,40},{12,28},{16,48},{20,4},{24,56},{28,12},{32,0}... | collective-permute-start | bytes 196616 | tf_op jit(solution)/shard_map/ppermute | solution.py:36
  41.7 5.3 %collective-permute-done.3 = bf16[8,128,128]{2,1,0:T(8,128)(2,1)S(1)} collective-permute-done((bf16[8,128,128]{2,1,0:T(8,128)(2,1)S(1)}, bf16[8,128,128]{2,1,0:T(8,128)(2,1)S(1)}, u32[]{:S(2)}, u32[]{:S(2)}) %collective-permute-start.3) | collective-permute-done | bytes 262176 | tf_op jit(solution)/shard_map/ppermute | solution.py:36
  51.7 48.9 %gather_fusion = s32[8192]{0:T(1024)S(1)} fusion(s32[128]{0:T(128)S(1)} %copy-done.2, s32[8192]{0:T(1024)S(1)} %fusion.50), kind=kCustom, calls=%fused_computation | custom fusion | bytes 98304 | tf_op jit(solution)/shard_map/jit(_take)/gather | solution.py:96
  105.0 2.7 collective-permute-done.9
  111.7 6.2 %collective-permute-done.10 = bf16[16,128,128]{2,1,0:T(8,128)(2,1)S(1)} collective-permute-done((bf16[16,128,128]{2,1,0:T(8,128)(2,1)S(1)}, bf16[16,128,128]{2,1,0:T(8,128)(2,1)S(1)}, u32[]{:S(2)}, u32[]{:S(2)}) %collective-permute-start.10) | collective-permute-done | bytes 524320 | tf_op jit(solution)/shard_map/ppermute | solution.py:36
  119.3 32.4 %while.32 = (s32[]{:T(128)}, f32[8,128]{1,0:T(8,128)S(1)}, f32[8,128]{1,0:T(8,128)S(1)}, s32[8192]{0:T(1024)S(1)}, s32[]{:T(128)}, /*index=5*/s32[128]{0:T(128)S...) while((s32[]{:T(128)}, f32[8,128]{1,0:T(8,128)S(1)}, ...), condition=%wide.region_8.9_spmd, body=%wide.region_2.0_spmd.sunk | while | flops 276958208 | bytes 9372437 | solution.py:157
  158.6 74.2 %while.33 = (s32[]{:T(128)}, f32[128,8,128]{2,0,1:T(8,128)S(1)}, f32[8192,128]{1,0:T(8,128)}, f32[8192,128]{1,0:T(8,128)}, s32[8192]{0:T(1024)S(1)}, /*index=5*/...) while((s32[]{:T(128)}, f32[128,8,128]{2,0,1:T(8,128)S(1)}, ...), condition=%wide.region_14.15_spmd, body=%wide.region_10.14_spmd.sunk | while | flops 1353974784 | bytes 23225780 | solution.py:168
  160.5 7.4 %conditional.5 = ((f32[128,8,128]{2,0,1:T(8,128)S(1)}, f32[8192,128]{1,0:T(8,128)}, f32[8192,128]{1,0:T(8,128)})) conditional(s32[]{:T(128)} %convert_element_type.102, (s32[1024]{0:T(1024)S(1)}, s32[128]{0:T(128)S(1)}, bf16[8192,128]{1,0:T(8,128)(2,1)S(1)}, s32[]{:T(128)}, bf16[128,8,128]{2,0,1:T(8,128)(2,1)S(1)}, ...), branch_computations={%region_12.12_spmd, %region_13.13_spmd} | conditional | flops 1353973760 | bytes 23217234 | solution.py:100
  161.4 2.5 fusion.7
  169.8 7.4 %conditional.5 = ((f32[128,8,128]{2,0,1:T(8,128)S(1)}, f32[8192,128]{1,0:T(8,128)}, f32[8192,128]{1,0:T(8,128)})) conditional(s32[]{:T(128)} %convert_element_type.102, (s32[1024]{0:T(1024)S(1)}, s32[128]{0:T(128)S(1)}, bf16[8192,128]{1,0:T(8,128)(2,1)S(1)}, s32[]{:T(128)}, bf16[128,8,128]{2,0,1:T(8,128)(2,1)S(1)}, ...), branch_computations={%region_12.12_spmd, %region_13.13_spmd} | conditional | flops 1353973760 | bytes 23217234 | solution.py:100
  179.1 7.3 %conditional.5 = ((f32[128,8,128]{2,0,1:T(8,128)S(1)}, f32[8192,128]{1,0:T(8,128)}, f32[8192,128]{1,0:T(8,128)})) conditional(s32[]{:T(128)} %convert_element_type.102, (s32[1024]{0:T(1024)S(1)}, s32[128]{0:T(128)S(1)}, bf16[8192,128]{1,0:T(8,128)(2,1)S(1)}, s32[]{:T(128)}, bf16[128,8,128]{2,0,1:T(8,128)(2,1)S(1)}, ...), branch_computations={%region_12.12_spmd, %region_13.13_spmd} | conditional | flops 1353973760 | bytes 23217234 | solution.py:100
  188.3 7.4 %conditional.5 = ((f32[128,8,128]{2,0,1:T(8,128)S(1)}, f32[8192,128]{1,0:T(8,128)}, f32[8192,128]{1,0:T(8,128)})) conditional(s32[]{:T(128)} %convert_element_type.102, (s32[1024]{0:T(1024)S(1)}, s32[128]{0:T(128)S(1)}, bf16[8192,128]{1,0:T(8,128)(2,1)S(1)}, s32[]{:T(128)}, bf16[128,8,128]{2,0,1:T(8,128)(2,1)S(1)}, ...), branch_computations={%region_12.12_spmd, %region_13.13_spmd} | conditional | flops 1353973760 | bytes 23217234 | solution.py:100
  197.6 7.4 %conditional.5 = ((f32[128,8,128]{2,0,1:T(8,128)S(1)}, f32[8192,128]{1,0:T(8,128)}, f32[8192,128]{1,0:T(8,128)})) conditional(s32[]{:T(128)} %convert_element_type.102, (s32[1024]{0:T(1024)S(1)}, s32[128]{0:T(128)S(1)}, bf16[8192,128]{1,0:T(8,128)(2,1)S(1)}, s32[]{:T(128)}, bf16[128,8,128]{2,0,1:T(8,128)(2,1)S(1)}, ...), branch_computations={%region_12.12_spmd, %region_13.13_spmd} | conditional | flops 1353973760 | bytes 23217234 | solution.py:100
  206.9 7.3 %conditional.5 = ((f32[128,8,128]{2,0,1:T(8,128)S(1)}, f32[8192,128]{1,0:T(8,128)}, f32[8192,128]{1,0:T(8,128)})) conditional(s32[]{:T(128)} %convert_element_type.102, (s32[1024]{0:T(1024)S(1)}, s32[128]{0:T(128)S(1)}, bf16[8192,128]{1,0:T(8,128)(2,1)S(1)}, s32[]{:T(128)}, bf16[128,8,128]{2,0,1:T(8,128)(2,1)S(1)}, ...), branch_computations={%region_12.12_spmd, %region_13.13_spmd} | conditional | flops 1353973760 | bytes 23217234 | solution.py:100
  216.1 7.4 %conditional.5 = ((f32[128,8,128]{2,0,1:T(8,128)S(1)}, f32[8192,128]{1,0:T(8,128)}, f32[8192,128]{1,0:T(8,128)})) conditional(s32[]{:T(128)} %convert_element_type.102, (s32[1024]{0:T(1024)S(1)}, s32[128]{0:T(128)S(1)}, bf16[8192,128]{1,0:T(8,128)(2,1)S(1)}, s32[]{:T(128)}, bf16[128,8,128]{2,0,1:T(8,128)(2,1)S(1)}, ...), branch_computations={%region_12.12_spmd, %region_13.13_spmd} | conditional | flops 1353973760 | bytes 23217234 | solution.py:100
  225.4 7.4 %conditional.5 = ((f32[128,8,128]{2,0,1:T(8,128)S(1)}, f32[8192,128]{1,0:T(8,128)}, f32[8192,128]{1,0:T(8,128)})) conditional(s32[]{:T(128)} %convert_element_type.102, (s32[1024]{0:T(1024)S(1)}, s32[128]{0:T(128)S(1)}, bf16[8192,128]{1,0:T(8,128)(2,1)S(1)}, s32[]{:T(128)}, bf16[128,8,128]{2,0,1:T(8,128)(2,1)S(1)}, ...), branch_computations={%region_12.12_spmd, %region_13.13_spmd} | conditional | flops 1353973760 | bytes 23217234 | solution.py:100
  226.3 2.5 fusion.7
  232.8 4.0 %fusion.63 = (f32[4096,128]{1,0:T(8,128)S(1)}, f32[4096,128]{1,0:T(8,128)S(1)}, f32[4096,128]{1,0:T(8,128)S(1)}, f32[4096,128]{1,0:T(8,128)S(1)}) fusion(f32[8192,128]{1,0:T(8,128)} %get-tuple-element.527, f32[8192,128]{1,0:T(8,128)} %get-tuple-element.526), kind=kLoop, calls=%fused_computation.152 | loop fusion | bytes 16777216 | tf_op jit(solution)/shard_map/slice | solution.py:46
  237.5 3.7 %collective-permute-done.18 = f32[32,128,128]{2,1,0:T(8,128)S(1)} collective-permute-done((f32[32,128,128]{2,1,0:T(8,128)S(1)}, f32[32,128,128]{2,1,0:T(8,128)S(1)}, u32[]{:S(2)}, u32[]{:S(2)}) %collective-permute-start.18) | collective-permute-done | bytes 2097184 | tf_op jit(solution)/shard_map/ppermute | solution.py:45
  246.7 9.8 %collective-permute-done.19 = f32[16,128,128]{2,1,0:T(8,128)S(1)} collective-permute-done((f32[16,128,128]{2,1,0:T(8,128)S(1)}, f32[16,128,128]{2,1,0:T(8,128)S(1)}, u32[]{:S(2)}, u32[]{:S(2)}) %collective-permute-start.19) | collective-permute-done | bytes 1048608 | tf_op jit(solution)/shard_map/ppermute | solution.py:45
  257.5 15.9 %collective-permute-done.13 = f32[16,128,128]{2,1,0:T(8,128)S(1)} collective-permute-done((f32[16,128,128]{2,1,0:T(8,128)S(1)}, f32[16,128,128]{2,1,0:T(8,128)S(1)}, u32[]{:S(2)}, u32[]{:S(2)}) %collective-permute-start.13) | collective-permute-done | bytes 1048608 | tf_op jit(solution)/shard_map/ppermute | solution.py:45
  278.0 8.2 %collective-permute-done.14 = f32[8,128,128]{2,1,0:T(8,128)} collective-permute-done((f32[8,128,128]{2,1,0:T(8,128)}, f32[8,128,128]{2,1,0:T(8,128)}, u32[]{:S(2)}, u32[]{:S(2)}) %collective-permute-start.14) | collective-permute-done | bytes 524320 | tf_op jit(solution)/shard_map/ppermute | solution.py:45
  287.3 2.8 collective-permute-start.15
  290.1 6.3 %fusion.65 = f32[128,4096]{1,0:T(8,128)S(1)} fusion(bf16[128,1024]{0,1:T(8,128)(2,1)S(1)} %bitcast.189, bf16[4096,1024]{1,0:T(8,128)(2,1)} %param.17), kind=kOutput, calls=%fused_computation.154 | convolution fusion | flops 1073741824 | bytes 10747904 | tf_op jit(solution)/shard_map/dot_general | solution.py:63
  297.6 5.6 %collective-permute-start.16 = (f32[2,128,128]{2,1,0:T(8,128)S(1)}, f32[2,128,128]{2,1,0:T(8,128)S(1)}, u32[]{:S(2)}, u32[]{:S(2)}) collective-permute-start(f32[2,128,128]{2,1,0:T(8,128)S(1)} %slice.121), channel_id=1, source_target_pairs={{0,32},{4,20},{8,40},{12,28},{16,48},{20,4},{24,56},{28,12},{32,0}... | collective-permute-start | bytes 393224 | tf_op jit(solution)/shard_map/ppermute | solution.py:45
  303.7 2.9 collective-permute-done.16
  306.7 5.7 %collective-permute-start.17 = (f32[1,128,128]{2,1,0:T(8,128)S(1)}, f32[1,128,128]{2,1,0:T(8,128)S(1)}, u32[]{:S(2)}, u32[]{:S(2)}) collective-permute-start(f32[1,128,128]{2,1,0:T(8,128)S(1)} %slice.123), channel_id=1, source_target_pairs={{0,128},{4,36},{8,136},{12,44},{16,144},{20,52},{24,152},{28,60},{... | collective-permute-start | bytes 196616 | tf_op jit(solution)/shard_map/ppermute | solution.py:45
  316.7 3.7 %collective-permute-done.23 = f32[1,128,128]{2,1,0:T(8,128)S(1)} collective-permute-done((f32[1,128,128]{2,1,0:T(8,128)S(1)}, f32[1,128,128]{2,1,0:T(8,128)S(1)}, u32[]{:S(2)}, u32[]{:S(2)}) %collective-permute-start.23) | collective-permute-done | bytes 65568 | tf_op jit(solution)/shard_map/ppermute | solution.py:45
  321.9 27.1 %reduce-scatter.2.cloned.1.call-done = bf16[128,1024]{1,0:T(8,128)(2,1)} async-done(((bf16[128,4096]{1,0:T(8,128)(2,1)}), bf16[128,1024]{1,0:T(8,128)(2,1)}) %reduce-scatter.2.cloned.1.call-update) | async-done | bytes 262160 | tf_op jit(solution)/shard_map/reduce_scatter | solution.py:176
  (229 shorter events, 154.1 us)
Async XLA Ops:
  6.5 342.5 %reduce-scatter.2.cloned.1.call-start = ((), (), s32[]{:S(2)}) async-start(), calls=%async_computation.1 | async-start | bytes 1310720 | tf_op jit(solution)/shard_map/reduce_scatter | solution.py:176
  7.8 4.5 %copy-start.4 = (bf16[4096,128]{1,0:T(8,128)(2,1)S(1)}, bf16[4096,128]{1,0:T(8,128)(2,1)}, u32[]{:S(2)}) copy-start(bf16[4096,128]{1,0:T(8,128)(2,1)} %param.19) | copy-start | bytes 3145732
  10.1 9.3 %collective-permute-start = (bf16[1,128,128]{2,1,0:T(8,128)(2,1)S(1)}, bf16[1,128,128]{2,1,0:T(8,128)(2,1)S(1)}, u32[]{:S(2)}, u32[]{:S(2)}) collective-permute-start(bf16[1,128,128]{2,1,0:T(8,128)(2,1)S(1)} %get-tuple-element.679), channel_id=1, source_target_pairs={{0,128},{4,36},{8,136},{12,44},{16,144},{20,52},{24,152},{28,60},{... | collective-permute-start | bytes 98312 | tf_op jit(solution)/shard_map/ppermute | solution.py:36
  13.4 20.9 %collective-permute-start.6 = (bf16[1,128,128]{2,1,0:T(8,128)(2,1)S(1)}, bf16[1,128,128]{2,1,0:T(8,128)(2,1)S(1)}, u32[]{:S(2)}, u32[]{:S(2)}) collective-permute-start(bf16[1,128,128]{2,1,0:T(8,128)(2,1)S(1)} %get-tuple-element.680), channel_id=1, source_target_pairs={{0,128},{4,36},{8,136},{12,44},{16,144},{20,52},{24,152},{28,60},{... | collective-permute-start | bytes 98312 | tf_op jit(solution)/shard_map/ppermute | solution.py:36
  19.4 9.6 %collective-permute-start.1 = (bf16[2,128,128]{2,1,0:T(8,128)(2,1)S(1)}, bf16[2,128,128]{2,1,0:T(8,128)(2,1)S(1)}, u32[]{:S(2)}, u32[]{:S(2)}) collective-permute-start(bf16[2,128,128]{2,1,0:T(8,128)(2,1)S(1)} %pad_maximum_fusion.4), channel_id=1, source_target_pairs={{0,32},{4,20},{8,40},{12,28},{16,48},{20,4},{24,56},{28,12},{32,0}... | collective-permute-start | bytes 196616 | tf_op jit(solution)/shard_map/ppermute | solution.py:36
  29.1 9.9 %collective-permute-start.2 = (bf16[4,128,128]{2,1,0:T(8,128)(2,1)S(1)}, bf16[4,128,128]{2,1,0:T(8,128)(2,1)S(1)}, u32[]{:S(2)}, u32[]{:S(2)}) collective-permute-start(bf16[4,128,128]{2,1,0:T(8,128)(2,1)S(1)} %pad_maximum_fusion.2), channel_id=1, source_target_pairs={{0,16},{4,132},{8,24},{12,140},{16,0},{20,148},{24,8},{28,156},{32... | collective-permute-start | bytes 393224 | tf_op jit(solution)/shard_map/ppermute | solution.py:36
  34.3 17.4 %copy-start.2 = (s32[128]{0:T(128)S(1)}, s32[128]{0:T(128)}, u32[]{:S(2)}) copy-start(s32[128]{0:T(128)} %param.22) | copy-start | bytes 1540
  34.3 15.7 %collective-permute-start.7 = (bf16[2,128,128]{2,1,0:T(8,128)(2,1)S(1)}, bf16[2,128,128]{2,1,0:T(8,128)(2,1)S(1)}, u32[]{:S(2)}, u32[]{:S(2)}) collective-permute-start(bf16[2,128,128]{2,1,0:T(8,128)(2,1)S(1)} %pad_maximum_fusion.5), channel_id=1, source_target_pairs={{0,32},{4,20},{8,40},{12,28},{16,48},{20,4},{24,56},{28,12},{32,0}... | collective-permute-start | bytes 196616 | tf_op jit(solution)/shard_map/ppermute | solution.py:36
  39.0 8.0 %collective-permute-start.3 = (bf16[8,128,128]{2,1,0:T(8,128)(2,1)S(1)}, bf16[8,128,128]{2,1,0:T(8,128)(2,1)S(1)}, u32[]{:S(2)}, u32[]{:S(2)}) collective-permute-start(bf16[8,128,128]{2,1,0:T(8,128)(2,1)S(1)} %pad_maximum_fusion), channel_id=1, source_target_pairs={{0,64},{4,12},{8,72},{12,4},{16,80},{20,28},{24,88},{28,20},{32,96... | collective-permute-start | bytes 786440 | tf_op jit(solution)/shard_map/ppermute | solution.py:36
  48.0 53.4 %collective-permute-start.4 = (bf16[16,128,128]{2,1,0:T(8,128)(2,1)}, bf16[16,128,128]{2,1,0:T(8,128)(2,1)}, u32[]{:S(2)}, u32[]{:S(2)}) collective-permute-start(bf16[16,128,128]{2,1,0:T(8,128)(2,1)} %get-tuple-element.654), channel_id=1, source_target_pairs={{0,8},{4,68},{8,0},{12,76},{16,24},{20,84},{24,16},{28,92},{32,40}... | collective-permute-start | bytes 1572872 | tf_op jit(solution)/shard_map/ppermute | solution.py:36
  50.0 51.2 %collective-permute-start.8 = (bf16[4,128,128]{2,1,0:T(8,128)(2,1)S(1)}, bf16[4,128,128]{2,1,0:T(8,128)(2,1)S(1)}, u32[]{:S(2)}, u32[]{:S(2)}) collective-permute-start(bf16[4,128,128]{2,1,0:T(8,128)(2,1)S(1)} %pad_maximum_fusion.3), channel_id=1, source_target_pairs={{0,16},{4,132},{8,24},{12,140},{16,0},{20,148},{24,8},{28,156},{32... | collective-permute-start | bytes 393224 | tf_op jit(solution)/shard_map/ppermute | solution.py:36
  101.3 2.3 copy-start.7
  101.3 6.5 %collective-permute-start.9 = (bf16[8,128,128]{2,1,0:T(8,128)(2,1)S(1)}, bf16[8,128,128]{2,1,0:T(8,128)(2,1)S(1)}, u32[]{:S(2)}, u32[]{:S(2)}) collective-permute-start(bf16[8,128,128]{2,1,0:T(8,128)(2,1)S(1)} %pad_maximum_fusion.1), channel_id=1, source_target_pairs={{0,64},{4,12},{8,72},{12,4},{16,80},{20,28},{24,88},{28,20},{32,96... | collective-permute-start | bytes 786440 | tf_op jit(solution)/shard_map/ppermute | solution.py:36
  103.6 15.5 %collective-permute-start.5 = (bf16[32,128,128]{2,1,0:T(8,128)(2,1)}, bf16[32,128,128]{2,1,0:T(8,128)(2,1)S(1)}, u32[]{:S(2)}, u32[]{:S(2)}) collective-permute-start(bf16[32,128,128]{2,1,0:T(8,128)(2,1)} %get-tuple-element.647), channel_id=1, source_target_pairs={{0,4},{4,0},{8,12},{12,8},{16,20},{20,16},{24,28},{28,24},{32,36},... | collective-permute-start | bytes 3145736 | tf_op jit(solution)/shard_map/ppermute | solution.py:36
  108.7 9.2 %collective-permute-start.10 = (bf16[16,128,128]{2,1,0:T(8,128)(2,1)S(1)}, bf16[16,128,128]{2,1,0:T(8,128)(2,1)S(1)}, u32[]{:S(2)}, u32[]{:S(2)}) collective-permute-start(bf16[16,128,128]{2,1,0:T(8,128)(2,1)S(1)} %get-tuple-element.651), channel_id=1, source_target_pairs={{0,8},{4,68},{8,0},{12,76},{16,24},{20,84},{24,16},{28,92},{32,40}... | collective-permute-start | bytes 1572872 | tf_op jit(solution)/shard_map/ppermute | solution.py:36
  119.1 32.6 %collective-permute-start.11 = (bf16[32,128,128]{2,1,0:T(8,128)(2,1)}, bf16[32,128,128]{2,1,0:T(8,128)(2,1)}, u32[]{:S(2)}, u32[]{:S(2)}) collective-permute-start(bf16[32,128,128]{2,1,0:T(8,128)(2,1)} %get-tuple-element.645), channel_id=1, source_target_pairs={{0,4},{4,0},{8,12},{12,8},{16,20},{20,16},{24,28},{28,24},{32,36},... | collective-permute-start | bytes 3145736 | tf_op jit(solution)/shard_map/ppermute | solution.py:36
  156.3 2.2 copy-start.6
  236.8 4.4 %collective-permute-start.18 = (f32[32,128,128]{2,1,0:T(8,128)S(1)}, f32[32,128,128]{2,1,0:T(8,128)S(1)}, u32[]{:S(2)}, u32[]{:S(2)}) collective-permute-start(f32[32,128,128]{2,1,0:T(8,128)S(1)} %bitcast.188), channel_id=1, source_target_pairs={{0,4},{4,0},{8,12},{12,8},{16,20},{20,16},{24,28},{28,24},{32,36},... | collective-permute-start | bytes 6291464 | tf_op jit(solution)/shard_map/ppermute | solution.py:45
  237.4 6.8 %collective-permute-start.12 = (f32[32,128,128]{2,1,0:T(8,128)S(1)}, f32[32,128,128]{2,1,0:T(8,128)S(1)}, u32[]{:S(2)}, u32[]{:S(2)}) collective-permute-start(f32[32,128,128]{2,1,0:T(8,128)S(1)} %bitcast.187), channel_id=1, source_target_pairs={{0,4},{4,0},{8,12},{12,8},{16,20},{20,16},{24,28},{28,24},{32,36},... | collective-permute-start | bytes 6291464 | tf_op jit(solution)/shard_map/ppermute | solution.py:45
  241.6 14.9 %collective-permute-start.19 = (f32[16,128,128]{2,1,0:T(8,128)S(1)}, f32[16,128,128]{2,1,0:T(8,128)S(1)}, u32[]{:S(2)}, u32[]{:S(2)}) collective-permute-start(f32[16,128,128]{2,1,0:T(8,128)S(1)} %slice.125), channel_id=1, source_target_pairs={{0,8},{4,68},{8,0},{12,76},{16,24},{20,84},{24,16},{28,92},{32,40}... | collective-permute-start | bytes 3145736 | tf_op jit(solution)/shard_map/ppermute | solution.py:45
  244.6 28.8 %collective-permute-start.13 = (f32[16,128,128]{2,1,0:T(8,128)S(1)}, f32[16,128,128]{2,1,0:T(8,128)S(1)}, u32[]{:S(2)}, u32[]{:S(2)}) collective-permute-start(f32[16,128,128]{2,1,0:T(8,128)S(1)} %slice.115), channel_id=1, source_target_pairs={{0,8},{4,68},{8,0},{12,76},{16,24},{20,84},{24,16},{28,92},{32,40}... | collective-permute-start | bytes 3145736 | tf_op jit(solution)/shard_map/ppermute | solution.py:45
  257.5 17.0 %collective-permute-start.20 = (f32[8,128,128]{2,1,0:T(8,128)}, f32[8,128,128]{2,1,0:T(8,128)}, u32[]{:S(2)}, u32[]{:S(2)}) collective-permute-start(f32[8,128,128]{2,1,0:T(8,128)} %slice.127), channel_id=1, source_target_pairs={{0,64},{4,12},{8,72},{12,4},{16,80},{20,28},{24,88},{28,20},{32,96... | collective-permute-start | bytes 1572872 | tf_op jit(solution)/shard_map/ppermute | solution.py:45
  274.3 11.9 %collective-permute-start.14 = (f32[8,128,128]{2,1,0:T(8,128)}, f32[8,128,128]{2,1,0:T(8,128)}, u32[]{:S(2)}, u32[]{:S(2)}) collective-permute-start(f32[8,128,128]{2,1,0:T(8,128)} %slice.117), channel_id=1, source_target_pairs={{0,64},{4,12},{8,72},{12,4},{16,80},{20,28},{24,88},{28,20},{32,96... | collective-permute-start | bytes 1572872 | tf_op jit(solution)/shard_map/ppermute | solution.py:45
  275.6 27.5 %collective-permute-start.21 = (f32[4,128,128]{2,1,0:T(8,128)S(1)}, f32[4,128,128]{2,1,0:T(8,128)S(1)}, u32[]{:S(2)}, u32[]{:S(2)}) collective-permute-start(f32[4,128,128]{2,1,0:T(8,128)S(1)} %slice.129), channel_id=1, source_target_pairs={{0,16},{4,132},{8,24},{12,140},{16,0},{20,148},{24,8},{28,156},{32... | collective-permute-start | bytes 786440 | tf_op jit(solution)/shard_map/ppermute | solution.py:45
  287.3 10.2 %collective-permute-start.15 = (f32[4,128,128]{2,1,0:T(8,128)S(1)}, f32[4,128,128]{2,1,0:T(8,128)S(1)}, u32[]{:S(2)}, u32[]{:S(2)}) collective-permute-start(f32[4,128,128]{2,1,0:T(8,128)S(1)} %slice.119), channel_id=1, source_target_pairs={{0,16},{4,132},{8,24},{12,140},{16,0},{20,148},{24,8},{28,156},{32... | collective-permute-start | bytes 786440 | tf_op jit(solution)/shard_map/ppermute | solution.py:45
  296.4 19.9 %copy-start.3 = (bf16[4096,128]{1,0:T(8,128)(2,1)S(1)}, bf16[4096,128]{1,0:T(8,128)(2,1)}, u32[]{:S(2)}) copy-start(bf16[4096,128]{1,0:T(8,128)(2,1)} %param.18) | copy-start | bytes 3145732
  297.6 9.1 %collective-permute-start.16 = (f32[2,128,128]{2,1,0:T(8,128)S(1)}, f32[2,128,128]{2,1,0:T(8,128)S(1)}, u32[]{:S(2)}, u32[]{:S(2)}) collective-permute-start(f32[2,128,128]{2,1,0:T(8,128)S(1)} %slice.121), channel_id=1, source_target_pairs={{0,32},{4,20},{8,40},{12,28},{16,48},{20,4},{24,56},{28,12},{32,0}... | collective-permute-start | bytes 393224 | tf_op jit(solution)/shard_map/ppermute | solution.py:45
  303.2 11.4 %collective-permute-start.22 = (f32[2,128,128]{2,1,0:T(8,128)S(1)}, f32[2,128,128]{2,1,0:T(8,128)S(1)}, u32[]{:S(2)}, u32[]{:S(2)}) collective-permute-start(f32[2,128,128]{2,1,0:T(8,128)S(1)} %slice.131), channel_id=1, source_target_pairs={{0,32},{4,20},{8,40},{12,28},{16,48},{20,4},{24,56},{28,12},{32,0}... | collective-permute-start | bytes 393224 | tf_op jit(solution)/shard_map/ppermute | solution.py:45
  306.7 9.6 %collective-permute-start.17 = (f32[1,128,128]{2,1,0:T(8,128)S(1)}, f32[1,128,128]{2,1,0:T(8,128)S(1)}, u32[]{:S(2)}, u32[]{:S(2)}) collective-permute-start(f32[1,128,128]{2,1,0:T(8,128)S(1)} %slice.123), channel_id=1, source_target_pairs={{0,128},{4,36},{8,136},{12,44},{16,144},{20,52},{24,152},{28,60},{... | collective-permute-start | bytes 196616 | tf_op jit(solution)/shard_map/ppermute | solution.py:45
  314.6 5.9 %copy-start.5 = (bf16[4096,128]{1,0:T(8,128)(2,1)S(1)}, bf16[4096,128]{1,0:T(8,128)(2,1)}, u32[]{:S(2)}) copy-start(bf16[4096,128]{1,0:T(8,128)(2,1)} %param.19) | copy-start | bytes 3145732
  314.6 5.9 %collective-permute-start.23 = (f32[1,128,128]{2,1,0:T(8,128)S(1)}, f32[1,128,128]{2,1,0:T(8,128)S(1)}, u32[]{:S(2)}, u32[]{:S(2)}) collective-permute-start(f32[1,128,128]{2,1,0:T(8,128)S(1)} %slice.133), channel_id=1, source_target_pairs={{0,128},{4,36},{8,136},{12,44},{16,144},{20,52},{24,152},{28,60},{... | collective-permute-start | bytes 196616 | tf_op jit(solution)/shard_map/ppermute | solution.py:45
  316.3 32.7 %copy-start.1 = (bf16[128,4096]{1,0:T(8,128)(2,1)S(1)}, bf16[128,4096]{1,0:T(8,128)(2,1)}, u32[]{:S(2)}) copy-start(bf16[128,4096]{1,0:T(8,128)(2,1)} %param.16) | copy-start | bytes 3145732
  (1 other events, 1.2 us)
Sparse Core Ops, SparseCore 0:
  322.0 26.9 reduce-scatter.1
